TPU v7x, 32 devices: a whole 2x2x4 slice. The times are simulated.
32 devices in a mesh: grp: 2 (over x), row: 16 (over z, y, core).
Axes of the slice: x: 2, y: 2, z: 4, core: 2. Of those that a mesh axis runs over, the one named last changes fastest.
Arguments:
- panels: bfloat16 [3, 8192, 1536], P(None, 'row'), may hold values from -0.099436891 to 0.099436891, as said below
- first_f: bfloat16 [1536, 512], P('row', 'grp'), parts along dimension 1, may hold values from -6 to 6
- first_g: bfloat16 [1536, 512], P('row', 'grp'), parts along dimension 1, may hold values from -6 to 6
- phase: float32 [4, 1536], P('grp'), parts along dimension 0, may hold values from -3.140625 to 3.140625
- wavenum: float32 [4, 1536], P('grp'), parts along dimension 0, may hold values from 0.5 to 2
Outputs:
- final_f: float32 [1536, 512], P('row', 'grp'), parts along dimension 1
- final_g: float32 [1536, 512], P('row', 'grp'), parts along dimension 1
There are 2 independent parts, one for each index of `grp`. A program takes and returns all parts, laid end to end along the dimension named above; an argument that names none is the same for every part. Nothing has to cross between parts.
Inputs may be any that keep to these rules, and one draw needn't show every extreme that they name: `panels`: consecutive sectors' surface functions share part of their shape.
All inputs are finite; a program needn't handle non-finite values.
Results may differ from a plain program's by a relative error of at most 0.013.
Values may be sent and summed in bfloat16 or wider, within the bound.
No kernel may reach another device: no remote copies, remote signals or barrier semaphores. Data moves between devices by JAX's collectives and lax.ppermute only.
A program may use at most 64 MiB of HBM per device.

v0:
```python
import jax
import jax.numpy as jnp
from jax import lax
from jax.sharding import PartitionSpec as P

SECTORS = 2


def contract_rows(left, right):
    return lax.dot_general(
        left, right, (((0,), (0,)), ((), ())), preferred_element_type=jnp.float32
    )


def shards(panels, first_f, first_g, phase, wavenum):
    chan_rows = first_f.shape[0]
    width = first_f.shape[1]
    all_channels = chan_rows * lax.axis_size("row")
    first_row = lax.axis_index("row") * chan_rows
    state = jnp.concatenate([first_f, first_g], axis=1).astype(jnp.float32)
    for sector in range(SECTORS):
        current = panels[sector]
        following = panels[sector + 1]
        solutions = state.astype(jnp.bfloat16)
        flipped = lax.psum_scatter(
            contract_rows(following, current), "row", scatter_dimension=0, tiled=True
        ).astype(jnp.bfloat16)
        rotated = jnp.dot(
            flipped,
            lax.all_gather(solutions, "row", axis=0, tiled=True),
            preferred_element_type=jnp.float32,
        )
        rot_amp = rotated[:, :width]
        rot_der = rotated[:, width:]
        angle_rows = lax.dynamic_slice_in_dim(phase[sector], first_row, chan_rows, 0)
        wave_rows = lax.dynamic_slice_in_dim(wavenum[sector], first_row, chan_rows, 0)
        cosine = jnp.cos(angle_rows)[:, None]
        sine = jnp.sin(angle_rows)[:, None]
        wave = wave_rows[:, None]
        new_amp = cosine * rot_amp + sine / wave * rot_der
        new_der = -wave * sine * rot_amp + cosine * rot_der
        local_norm = jnp.sum(new_amp * new_amp, axis=0) + jnp.sum(new_der * new_der, axis=0)
        norm = lax.psum(local_norm, "row")
        scale = 1.0 / jnp.sqrt(norm / (2.0 * all_channels) + 1e-06)
        state = jnp.concatenate([new_amp * scale[None, :], new_der * scale[None, :]], axis=1)
    return (state[:, :width], state[:, width:])


def solution(mesh):
    in_specs = (
        P(None, "row", None),
        P("row", "grp"),
        P("row", "grp"),
        P("grp", None),
        P("grp", None),
    )
    out_specs = (P("row", "grp"), P("row", "grp"))
    return jax.shard_map(shards, mesh=mesh, in_specs=in_specs, out_specs=out_specs, check_vma=False)
```

profile of v0, /device:TPU:0, one launch (start us, length us, event | category | flops | bytes accessed | tf_op | source)
XLA Modules:
  0.0 366.6 jit_solution(17294964851320102471)
XLA Ops:
  7.2 0.0 all-gather.3.cloned.1.call-start
  7.2 1.5 pad_maximum_fusion
  8.7 0.0 all-gather.3.cloned.1.call-update
  8.7 0.0 reduce-scatter.5.cloned.1.call-start
  8.8 8.2 %fusion = f32[1536,1536]{1,0:T(8,128)} fusion(bf16[3,512,1536]{2,1,0:T(8,128)(2,1)} %param.5), kind=kOutput, calls=%fused_computation | convolution fusion | flops 2415919104 | bytes 12582912 | tf_op jit(solution)/shard_map/dot_general | solution.py:10
  16.9 0.0 reduce-scatter.5.cloned.1.call-update
  17.0 0.0 reduce-scatter.3.cloned.1.call-start
  17.0 8.2 %fusion.3 = f32[1536,1536]{1,0:T(8,128)} fusion(bf16[3,512,1536]{2,1,0:T(8,128)(2,1)} %param.5), kind=kOutput, calls=%fused_computation.3 | convolution fusion | flops 2415919104 | bytes 12582912 | tf_op jit(solution)/shard_map/dot_general | solution.py:10
  25.2 0.0 copy-start
  25.2 0.0 copy-start.1
  25.2 0.0 reduce-scatter.3.cloned.1.call-update
  25.2 0.0 all-gather.5.cloned.1.call-start
  25.3 0.6 copy-done
  25.9 0.0 copy-done.1
  25.9 0.1 cosine_bitcast_fusion
  26.0 0.1 bitcast_divide_fusion.1
  26.2 27.1 %all-gather.3.cloned.1.call-done = bf16[1536,512]{1,0:T(8,128)(2,1)} async-done(((bf16[96,512]{1,0:T(8,128)(2,1)}), bf16[1536,512]{1,0:T(8,128)(2,1)}) %all-gather.3.cloned.1.call-update) | async-done | bytes 1572880 | tf_op jit(solution)/shard_map/all_gather | solution.py:30
  53.3 114.4 %reduce-scatter.5.cloned.1.call-done = f32[96,1536]{1,0:T(8,128)} async-done(((f32[1536,1536]{1,0:T(8,128)}), f32[96,1536]{1,0:T(8,128)}) %reduce-scatter.5.cloned.1.call-update) | async-done | bytes 589840 | tf_op jit(solution)/shard_map/reduce_scatter | solution.py:25
  167.6 2.0 fusion.10
  169.6 0.1 multiply_reduce_fusion.2
  169.7 32.2 %psum.14 = f32[256]{0:T(256)S(1)} all-reduce(f32[256]{0:T(256)S(1)} %add.41), channel_id=1, replica_groups=mesh['grp'=2,'row'=16] {'row'}, use_global_device_ids=true, to_apply=%region_4.0 | all-reduce | flops 256 | bytes 2048 | tf_op jit(solution)/shard_map/psum | solution.py:43
  202.0 0.1 multiply_convert_fusion.1
  202.1 0.6 pad_maximum_fusion.1
  202.7 0.0 all-gather.5.cloned.1.call-update
  202.8 0.1 cosine_bitcast_fusion.1
  202.9 0.1 bitcast_divide_fusion
  203.0 80.4 %reduce-scatter.3.cloned.1.call-done = f32[96,1536]{1,0:T(8,128)} async-done(((f32[1536,1536]{1,0:T(8,128)}), f32[96,1536]{1,0:T(8,128)}) %reduce-scatter.3.cloned.1.call-update) | async-done | bytes 589840 | tf_op jit(solution)/shard_map/reduce_scatter | solution.py:25
  283.4 42.2 %all-gather.5.cloned.1.call-done = bf16[1536,512]{1,0:T(8,128)(2,1)} async-done(((bf16[96,512]{1,0:T(8,128)(2,1)}), bf16[1536,512]{1,0:T(8,128)(2,1)}) %all-gather.5.cloned.1.call-update) | async-done | bytes 1572880 | tf_op jit(solution)/shard_map/all_gather | solution.py:30
  325.6 2.0 fusion.12
  327.6 0.1 multiply_reduce_fusion
  327.7 31.6 %psum.15 = f32[256]{0:T(256)S(1)} all-reduce(f32[256]{0:T(256)S(1)} %add.45), channel_id=1, replica_groups=mesh['grp'=2,'row'=16] {'row'}, use_global_device_ids=true, to_apply=%region_7.0 | all-reduce | flops 256 | bytes 2048 | tf_op jit(solution)/shard_map/psum | solution.py:43
  359.3 0.8 broadcast_multiply_fusion
  (5 shorter events, 0.0 us)
Async XLA Ops:
  7.2 46.1 %all-gather.3.cloned.1.call-start = ((), (), s32[]{:S(2)}) async-start(), calls=%async_computation.4 | async-start | bytes 1671168 | tf_op jit(solution)/shard_map/all_gather | solution.py:30
  8.7 158.9 %reduce-scatter.5.cloned.1.call-start = ((), (), s32[]{:S(2)}) async-start(), calls=%async_computation.3 | async-start | bytes 10027008 | tf_op jit(solution)/shard_map/reduce_scatter | solution.py:25
  17.0 266.4 %reduce-scatter.3.cloned.1.call-start = ((), (), s32[]{:S(2)}) async-start(), calls=%async_computation.2 | async-start | bytes 10027008 | tf_op jit(solution)/shard_map/reduce_scatter | solution.py:25
  25.2 0.7 copy-start
  25.2 0.7 copy-start.1
  25.2 300.4 %all-gather.5.cloned.1.call-start = ((), (), s32[]{:S(2)}) async-start(), calls=%async_computation.5 | async-start | bytes 1671168 | tf_op jit(solution)/shard_map/all_gather | solution.py:30
Sparse Core Ops, SparseCore 0:
  10.9 42.3 all-gather.2
  57.4 110.2 reduce-scatter.4
  172.3 111.0 reduce-scatter.2
  286.1 39.4 all-gather.4
where the time goes:
time: 367 us
  waiting for transfers between devices  264 us (72%)
  blocking collectives  63.8 us (17%)
  matrix products  20.3 us (6%)
  between operations  13.8 us (4%)
    reduce_scatter x2, waiting for transfers between devices, shards(): lax.psum_scatter(contract_rows(following, current), 'row', scatter_dimens...  195 us
    all_gather x2, waiting for transfers between devices, shards(): lax.all_gather(solutions, 'row', axis=0, tiled=True)  69.3 us
    psum x2, blocking collectives, shards(): norm = lax.psum(local_norm, 'row')  63.8 us
    dot_general x2, matrix products, contract_rows(): lax.dot_general(left, right, (((0,), (0,)), ((), ())), preferred_element_...  16.3 us
  transfers between devices with their start and end apart: 4, of which 4 were waited for; matrix products, arithmetic and copies ran while one was open for 5% of the time, Pallas kernels for 0%

commit v1 on v0

--- a/solution.py
+++ b/solution.py
@@ -4,6 +4,16 @@
 from jax.sharding import PartitionSpec as P
 
 SECTORS = 2
+
+
+def ring_gather(x, axis, dim):
+    ways, here, step = (lax.axis_size(axis), lax.axis_index(axis), x.shape[dim])
+    lengths = [n * ways if d == dim else n for d, n in enumerate(x.shape)]
+    full = lax.dynamic_update_slice_in_dim(jnp.zeros(lengths, x.dtype), x, here * step, axis=dim)
+    for far in range(1, ways):
+        x = lax.ppermute(x, axis, [(d, (d + 1) % ways) for d in range(ways)])
+        full = lax.dynamic_update_slice_in_dim(full, x, (here - far) % ways * step, axis=dim)
+    return full
 
 
 def contract_rows(left, right):
@@ -26,9 +36,7 @@
             contract_rows(following, current), "row", scatter_dimension=0, tiled=True
         ).astype(jnp.bfloat16)
         rotated = jnp.dot(
-            flipped,
-            lax.all_gather(solutions, "row", axis=0, tiled=True),
-            preferred_element_type=jnp.float32,
+            flipped, ring_gather(solutions, "row", 0), preferred_element_type=jnp.float32
         )
         rot_amp = rotated[:, :width]
         rot_der = rotated[:, width:]

time: 367 us -> 330 us (0.90)
  waiting for transfers between devices: 264 us -> 233 us
  blocking collectives: 63.8 us -> 59 us
    ppermute x0 -> x30, waiting for transfers between devices: none -> 233 us  [ring_gather(): x = lax.ppermute(x, axis, [(d, (d + 1) % ways) for d in range(ways)])]
    reduce_scatter x2, waiting for transfers between devices: 195 us -> 0.04 us  [shards(): lax.psum_scatter(contract_rows(following, current), 'row', scatter_dimens...]
    all_gather x2 -> x0, waiting for transfers between devices: 69.3 us -> none  [shards(): lax.all_gather(solutions, 'row', axis=0, tiled=True)]
    psum x2, blocking collectives: 63.8 us -> 59 us  [shards(): norm = lax.psum(local_norm, 'row')]
  transfers between devices with their start and end apart: 4 -> 32, of which waited for: 4 -> 30; matrix products, arithmetic and copies ran while one was open for 5% -> 3% of each run, Pallas kernels for 0% -> 0%
where the time goes in v1:
time: 330 us
  waiting for transfers between devices  233 us (71%)
  blocking collectives  59 us (18%)
  matrix products  19.3 us (6%)
  between operations  14.3 us (4%)
    ppermute x30, waiting for transfers between devices, ring_gather(): x = lax.ppermute(x, axis, [(d, (d + 1) % ways) for d in range(ways)])  233 us
    psum x2, blocking collectives, shards(): norm = lax.psum(local_norm, 'row')  59 us
    dot_general x2, matrix products, contract_rows(): lax.dot_general(left, right, (((0,), (0,)), ((), ())), preferred_element_...  16.4 us
  transfers between devices with their start and end apart: 32, of which 30 were waited for; matrix products, arithmetic and copies ran while one was open for 3% of the time, Pallas kernels for 0%

profile of v1, /device:TPU:0, one launch (start us, length us, event | category | flops | bytes accessed | tf_op | source)
XLA Modules:
  0.0 329.7 jit_solution(10051215555196242639)
XLA Ops:
  7.2 0.0 reduce-scatter.5.cloned.1.call-start
  7.2 8.2 %fusion = f32[1536,1536]{1,0:T(8,128)} fusion(bf16[3,512,1536]{2,1,0:T(8,128)(2,1)} %param.5), kind=kOutput, calls=%fused_computation | convolution fusion | flops 2415919104 | bytes 12582912 | tf_op jit(solution)/shard_map/dot_general | solution.py:20
  15.4 0.0 reduce-scatter.5.cloned.1.call-update
  15.5 0.0 reduce-scatter.3.cloned.1.call-start
  15.5 8.2 %fusion.3 = f32[1536,1536]{1,0:T(8,128)} fusion(bf16[3,512,1536]{2,1,0:T(8,128)(2,1)} %param.5), kind=kOutput, calls=%fused_computation.3 | convolution fusion | flops 2415919104 | bytes 12582912 | tf_op jit(solution)/shard_map/dot_general | solution.py:20
  23.7 0.0 reduce-scatter.3.cloned.1.call-update
  23.7 0.8 copy-done
  24.5 0.0 copy-done.1
  24.5 0.5 collective-permute-start
  25.0 0.1 bitcast_divide_fusion.1
  25.1 0.1 bitcast_divide_fusion
  25.3 0.1 broadcast.29.clone
  25.4 0.1 cosine_bitcast_fusion
  25.5 6.8 %collective-permute-done = bf16[96,512]{1,0:T(8,128)(2,1)S(1)} collective-permute-done((bf16[96,512]{1,0:T(8,128)(2,1)S(1)}, bf16[96,512]{1,0:T(8,128)(2,1)S(1)}, u32[]{:S(2)}, u32[]{:S(2)}) %collective-permute-start) | collective-permute-done | bytes 98336 | tf_op jit(solution)/shard_map/ppermute | solution.py:14
  32.3 0.0 collective-permute-start.1
  32.3 6.7 %collective-permute-done.1 = bf16[96,512]{1,0:T(8,128)(2,1)S(1)} collective-permute-done((bf16[96,512]{1,0:T(8,128)(2,1)S(1)}, bf16[96,512]{1,0:T(8,128)(2,1)S(1)}, u32[]{:S(2)}, u32[]{:S(2)}) %collective-permute-start.1) | collective-permute-done | bytes 98336 | tf_op jit(solution)/shard_map/ppermute | solution.py:14
  39.1 6.7 %collective-permute-done.2 = bf16[96,512]{1,0:T(8,128)(2,1)S(1)} collective-permute-done((bf16[96,512]{1,0:T(8,128)(2,1)S(1)}, bf16[96,512]{1,0:T(8,128)(2,1)S(1)}, u32[]{:S(2)}, u32[]{:S(2)}) %collective-permute-start.2) | collective-permute-done | bytes 98336 | tf_op jit(solution)/shard_map/ppermute | solution.py:14
  45.8 0.0 collective-permute-start.3
  45.8 6.7 %collective-permute-done.3 = bf16[96,512]{1,0:T(8,128)(2,1)S(1)} collective-permute-done((bf16[96,512]{1,0:T(8,128)(2,1)S(1)}, bf16[96,512]{1,0:T(8,128)(2,1)S(1)}, u32[]{:S(2)}, u32[]{:S(2)}) %collective-permute-start.3) | collective-permute-done | bytes 98336 | tf_op jit(solution)/shard_map/ppermute | solution.py:14
  52.5 0.0 collective-permute-start.4
  52.5 8.8 %collective-permute-done.4 = bf16[96,512]{1,0:T(8,128)(2,1)S(1)} collective-permute-done((bf16[96,512]{1,0:T(8,128)(2,1)S(1)}, bf16[96,512]{1,0:T(8,128)(2,1)S(1)}, u32[]{:S(2)}, u32[]{:S(2)}) %collective-permute-start.4) | collective-permute-done | bytes 98336 | tf_op jit(solution)/shard_map/ppermute | solution.py:14
  61.3 0.0 collective-permute-start.5
  61.4 8.8 %collective-permute-done.5 = bf16[96,512]{1,0:T(8,128)(2,1)S(1)} collective-permute-done((bf16[96,512]{1,0:T(8,128)(2,1)S(1)}, bf16[96,512]{1,0:T(8,128)(2,1)S(1)}, u32[]{:S(2)}, u32[]{:S(2)}) %collective-permute-start.5) | collective-permute-done | bytes 98336 | tf_op jit(solution)/shard_map/ppermute | solution.py:14
  70.2 0.0 collective-permute-start.6
  70.2 9.0 %collective-permute-done.6 = bf16[96,512]{1,0:T(8,128)(2,1)S(1)} collective-permute-done((bf16[96,512]{1,0:T(8,128)(2,1)S(1)}, bf16[96,512]{1,0:T(8,128)(2,1)S(1)}, u32[]{:S(2)}, u32[]{:S(2)}) %collective-permute-start.6) | collective-permute-done | bytes 98336 | tf_op jit(solution)/shard_map/ppermute | solution.py:14
  79.2 9.0 %collective-permute-done.7 = bf16[96,512]{1,0:T(8,128)(2,1)S(1)} collective-permute-done((bf16[96,512]{1,0:T(8,128)(2,1)S(1)}, bf16[96,512]{1,0:T(8,128)(2,1)S(1)}, u32[]{:S(2)}, u32[]{:S(2)}) %collective-permute-start.7) | collective-permute-done | bytes 98336 | tf_op jit(solution)/shard_map/ppermute | solution.py:14
  88.3 9.0 %collective-permute-done.8 = bf16[96,512]{1,0:T(8,128)(2,1)S(1)} collective-permute-done((bf16[96,512]{1,0:T(8,128)(2,1)S(1)}, bf16[96,512]{1,0:T(8,128)(2,1)S(1)}, u32[]{:S(2)}, u32[]{:S(2)}) %collective-permute-start.8) | collective-permute-done | bytes 98336 | tf_op jit(solution)/shard_map/ppermute | solution.py:14
  97.3 6.8 %collective-permute-done.9 = bf16[96,512]{1,0:T(8,128)(2,1)S(1)} collective-permute-done((bf16[96,512]{1,0:T(8,128)(2,1)S(1)}, bf16[96,512]{1,0:T(8,128)(2,1)S(1)}, u32[]{:S(2)}, u32[]{:S(2)}) %collective-permute-start.9) | collective-permute-done | bytes 98336 | tf_op jit(solution)/shard_map/ppermute | solution.py:14
  104.1 0.0 collective-permute-start.10
  104.1 6.7 %collective-permute-done.10 = bf16[96,512]{1,0:T(8,128)(2,1)S(1)} collective-permute-done((bf16[96,512]{1,0:T(8,128)(2,1)S(1)}, bf16[96,512]{1,0:T(8,128)(2,1)S(1)}, u32[]{:S(2)}, u32[]{:S(2)}) %collective-permute-start.10) | collective-permute-done | bytes 98336 | tf_op jit(solution)/shard_map/ppermute | solution.py:14
  110.9 0.0 collective-permute-start.11
  110.9 6.9 %collective-permute-done.11 = bf16[96,512]{1,0:T(8,128)(2,1)S(1)} collective-permute-done((bf16[96,512]{1,0:T(8,128)(2,1)S(1)}, bf16[96,512]{1,0:T(8,128)(2,1)S(1)}, u32[]{:S(2)}, u32[]{:S(2)}) %collective-permute-start.11) | collective-permute-done | bytes 98336 | tf_op jit(solution)/shard_map/ppermute | solution.py:14
  117.8 0.0 collective-permute-start.12
  117.8 8.9 %collective-permute-done.12 = bf16[96,512]{1,0:T(8,128)(2,1)S(1)} collective-permute-done((bf16[96,512]{1,0:T(8,128)(2,1)S(1)}, bf16[96,512]{1,0:T(8,128)(2,1)S(1)}, u32[]{:S(2)}, u32[]{:S(2)}) %collective-permute-start.12) | collective-permute-done | bytes 98336 | tf_op jit(solution)/shard_map/ppermute | solution.py:14
  126.7 9.0 %collective-permute-done.13 = bf16[96,512]{1,0:T(8,128)(2,1)S(1)} collective-permute-done((bf16[96,512]{1,0:T(8,128)(2,1)S(1)}, bf16[96,512]{1,0:T(8,128)(2,1)S(1)}, u32[]{:S(2)}, u32[]{:S(2)}) %collective-permute-start.13) | collective-permute-done | bytes 98336 | tf_op jit(solution)/shard_map/ppermute | solution.py:14
  135.7 6.7 %collective-permute-done.14 = bf16[96,512]{1,0:T(8,128)(2,1)S(1)} collective-permute-done((bf16[96,512]{1,0:T(8,128)(2,1)S(1)}, bf16[96,512]{1,0:T(8,128)(2,1)S(1)}, u32[]{:S(2)}, u32[]{:S(2)}) %collective-permute-start.14) | collective-permute-done | bytes 98336 | tf_op jit(solution)/shard_map/ppermute | solution.py:14
  142.5 0.0 reduce-scatter.5.cloned.1.call-done
  142.5 1.4 fusion.10
  144.0 0.1 multiply_reduce_fusion.2
  144.1 29.5 %psum.14 = f32[256]{0:T(256)S(1)} all-reduce(f32[256]{0:T(256)S(1)} %add.209), channel_id=1, replica_groups=mesh['grp'=2,'row'=16] {'row'}, use_global_device_ids=true, to_apply=%region_4.5 | all-reduce | flops 256 | bytes 2048 | tf_op jit(solution)/shard_map/psum | solution.py:51
  173.6 0.1 multiply_convert_fusion.1
  173.7 0.1 broadcast.29
  173.9 0.1 collective-permute-start.15
  173.9 0.1 cosine_bitcast_fusion.1
  174.1 8.6 %collective-permute-done.15 = bf16[96,512]{1,0:T(8,128)(2,1)S(1)} collective-permute-done((bf16[96,512]{1,0:T(8,128)(2,1)S(1)}, bf16[96,512]{1,0:T(8,128)(2,1)S(1)}, u32[]{:S(2)}, u32[]{:S(2)}) %collective-permute-start.15) | collective-permute-done | bytes 98336 | tf_op jit(solution)/shard_map/ppermute | solution.py:14
  182.7 8.8 %collective-permute-done.16 = bf16[96,512]{1,0:T(8,128)(2,1)S(1)} collective-permute-done((bf16[96,512]{1,0:T(8,128)(2,1)S(1)}, bf16[96,512]{1,0:T(8,128)(2,1)S(1)}, u32[]{:S(2)}, u32[]{:S(2)}) %collective-permute-start.16) | collective-permute-done | bytes 98336 | tf_op jit(solution)/shard_map/ppermute | solution.py:14
  191.5 9.0 %collective-permute-done.17 = bf16[96,512]{1,0:T(8,128)(2,1)S(1)} collective-permute-done((bf16[96,512]{1,0:T(8,128)(2,1)S(1)}, bf16[96,512]{1,0:T(8,128)(2,1)S(1)}, u32[]{:S(2)}, u32[]{:S(2)}) %collective-permute-start.17) | collective-permute-done | bytes 98336 | tf_op jit(solution)/shard_map/ppermute | solution.py:14
  200.6 9.0 %collective-permute-done.18 = bf16[96,512]{1,0:T(8,128)(2,1)S(1)} collective-permute-done((bf16[96,512]{1,0:T(8,128)(2,1)S(1)}, bf16[96,512]{1,0:T(8,128)(2,1)S(1)}, u32[]{:S(2)}, u32[]{:S(2)}) %collective-permute-start.18) | collective-permute-done | bytes 98336 | tf_op jit(solution)/shard_map/ppermute | solution.py:14
  209.6 9.0 %collective-permute-done.19 = bf16[96,512]{1,0:T(8,128)(2,1)S(1)} collective-permute-done((bf16[96,512]{1,0:T(8,128)(2,1)S(1)}, bf16[96,512]{1,0:T(8,128)(2,1)S(1)}, u32[]{:S(2)}, u32[]{:S(2)}) %collective-permute-start.19) | collective-permute-done | bytes 98336 | tf_op jit(solution)/shard_map/ppermute | solution.py:14
  218.7 6.8 %collective-permute-done.20 = bf16[96,512]{1,0:T(8,128)(2,1)S(1)} collective-permute-done((bf16[96,512]{1,0:T(8,128)(2,1)S(1)}, bf16[96,512]{1,0:T(8,128)(2,1)S(1)}, u32[]{:S(2)}, u32[]{:S(2)}) %collective-permute-start.20) | collective-permute-done | bytes 98336 | tf_op jit(solution)/shard_map/ppermute | solution.py:14
  225.5 6.7 %collective-permute-done.21 = bf16[96,512]{1,0:T(8,128)(2,1)S(1)} collective-permute-done((bf16[96,512]{1,0:T(8,128)(2,1)S(1)}, bf16[96,512]{1,0:T(8,128)(2,1)S(1)}, u32[]{:S(2)}, u32[]{:S(2)}) %collective-permute-start.21) | collective-permute-done | bytes 98336 | tf_op jit(solution)/shard_map/ppermute | solution.py:14
  232.2 6.7 %collective-permute-done.22 = bf16[96,512]{1,0:T(8,128)(2,1)S(1)} collective-permute-done((bf16[96,512]{1,0:T(8,128)(2,1)S(1)}, bf16[96,512]{1,0:T(8,128)(2,1)S(1)}, u32[]{:S(2)}, u32[]{:S(2)}) %collective-permute-start.22) | collective-permute-done | bytes 98336 | tf_op jit(solution)/shard_map/ppermute | solution.py:14
  239.0 8.8 %collective-permute-done.23 = bf16[96,512]{1,0:T(8,128)(2,1)S(1)} collective-permute-done((bf16[96,512]{1,0:T(8,128)(2,1)S(1)}, bf16[96,512]{1,0:T(8,128)(2,1)S(1)}, u32[]{:S(2)}, u32[]{:S(2)}) %collective-permute-start.23) | collective-permute-done | bytes 98336 | tf_op jit(solution)/shard_map/ppermute | solution.py:14
  247.8 9.0 %collective-permute-done.24 = bf16[96,512]{1,0:T(8,128)(2,1)S(1)} collective-permute-done((bf16[96,512]{1,0:T(8,128)(2,1)S(1)}, bf16[96,512]{1,0:T(8,128)(2,1)S(1)}, u32[]{:S(2)}, u32[]{:S(2)}) %collective-permute-start.24) | collective-permute-done | bytes 98336 | tf_op jit(solution)/shard_map/ppermute | solution.py:14
  256.8 7.2 %collective-permute-done.25 = bf16[96,512]{1,0:T(8,128)(2,1)S(1)} collective-permute-done((bf16[96,512]{1,0:T(8,128)(2,1)S(1)}, bf16[96,512]{1,0:T(8,128)(2,1)S(1)}, u32[]{:S(2)}, u32[]{:S(2)}) %collective-permute-start.25) | collective-permute-done | bytes 98336 | tf_op jit(solution)/shard_map/ppermute | solution.py:14
  264.0 6.7 %collective-permute-done.26 = bf16[96,512]{1,0:T(8,128)(2,1)S(1)} collective-permute-done((bf16[96,512]{1,0:T(8,128)(2,1)S(1)}, bf16[96,512]{1,0:T(8,128)(2,1)S(1)}, u32[]{:S(2)}, u32[]{:S(2)}) %collective-permute-start.26) | collective-permute-done | bytes 98336 | tf_op jit(solution)/shard_map/ppermute | solution.py:14
  270.8 6.7 %collective-permute-done.27 = bf16[96,512]{1,0:T(8,128)(2,1)S(1)} collective-permute-done((bf16[96,512]{1,0:T(8,128)(2,1)S(1)}, bf16[96,512]{1,0:T(8,128)(2,1)S(1)}, u32[]{:S(2)}, u32[]{:S(2)}) %collective-permute-start.27) | collective-permute-done | bytes 98336 | tf_op jit(solution)/shard_map/ppermute | solution.py:14
  277.5 6.7 %collective-permute-done.28 = bf16[96,512]{1,0:T(8,128)(2,1)S(1)} collective-permute-done((bf16[96,512]{1,0:T(8,128)(2,1)S(1)}, bf16[96,512]{1,0:T(8,128)(2,1)S(1)}, u32[]{:S(2)}, u32[]{:S(2)}) %collective-permute-start.28) | collective-permute-done | bytes 98336 | tf_op jit(solution)/shard_map/ppermute | solution.py:14
  284.2 6.7 %collective-permute-done.29 = bf16[96,512]{1,0:T(8,128)(2,1)S(1)} collective-permute-done((bf16[96,512]{1,0:T(8,128)(2,1)S(1)}, bf16[96,512]{1,0:T(8,128)(2,1)S(1)}, u32[]{:S(2)}, u32[]{:S(2)}) %collective-permute-start.29) | collective-permute-done | bytes 98336 | tf_op jit(solution)/shard_map/ppermute | solution.py:14
  291.0 0.0 reduce-scatter.3.cloned.1.call-done
  291.0 1.4 fusion.12
  292.5 0.1 multiply_reduce_fusion
  292.6 29.5 %psum.15 = f32[256]{0:T(256)S(1)} all-reduce(f32[256]{0:T(256)S(1)} %add.213), channel_id=1, replica_groups=mesh['grp'=2,'row'=16] {'row'}, use_global_device_ids=true, to_apply=%region_7.8 | all-reduce | flops 256 | bytes 2048 | tf_op jit(solution)/shard_map/psum | solution.py:51
  322.1 0.8 broadcast_multiply_fusion
  (65 shorter events, 0.5 us)
Async XLA Ops:
  7.2 135.3 %reduce-scatter.5.cloned.1.call-start = ((), (), s32[]{:S(2)}) async-start(), calls=%async_computation.3 | async-start | bytes 10027008 | tf_op jit(solution)/shard_map/reduce_scatter | solution.py:35
  15.5 275.6 %reduce-scatter.3.cloned.1.call-start = ((), (), s32[]{:S(2)}) async-start(), calls=%async_computation.2 | async-start | bytes 10027008 | tf_op jit(solution)/shard_map/reduce_scatter | solution.py:35
  23.7 0.8 copy-start
  23.7 0.8 copy-start.1
  23.7 1.3 copy-start.2
  23.7 1.3 copy-start.3
  24.5 7.8 %collective-permute-start = (bf16[96,512]{1,0:T(8,128)(2,1)S(1)}, bf16[96,512]{1,0:T(8,128)(2,1)S(1)}, u32[]{:S(2)}, u32[]{:S(2)}) collective-permute-start(bf16[96,512]{1,0:T(8,128)(2,1)S(1)} %constant_dynamic-update-slice_fusion.32), channel_id=1, source_target_pairs={{0,1},{1,2},{2,3},{3,4},{4,5},{5,6},{6,7},{7,8},{8,9},{9,10},{10,1... | collective-permute-start | bytes 294920 | tf_op jit(solution)/shard_map/ppermute | solution.py:14
  32.3 6.7 %collective-permute-start.1 = (bf16[96,512]{1,0:T(8,128)(2,1)S(1)}, bf16[96,512]{1,0:T(8,128)(2,1)S(1)}, u32[]{:S(2)}, u32[]{:S(2)}) collective-permute-start(bf16[96,512]{1,0:T(8,128)(2,1)S(1)} %collective-permute-done), channel_id=1, source_target_pairs={{0,1},{1,2},{2,3},{3,4},{4,5},{5,6},{6,7},{7,8},{8,9},{9,10},{10,1... | collective-permute-start | bytes 294920 | tf_op jit(solution)/shard_map/ppermute | solution.py:14
  39.0 6.7 %collective-permute-start.2 = (bf16[96,512]{1,0:T(8,128)(2,1)S(1)}, bf16[96,512]{1,0:T(8,128)(2,1)S(1)}, u32[]{:S(2)}, u32[]{:S(2)}) collective-permute-start(bf16[96,512]{1,0:T(8,128)(2,1)S(1)} %collective-permute-done.1), channel_id=1, source_target_pairs={{0,1},{1,2},{2,3},{3,4},{4,5},{5,6},{6,7},{7,8},{8,9},{9,10},{10,1... | collective-permute-start | bytes 294920 | tf_op jit(solution)/shard_map/ppermute | solution.py:14
  45.8 6.7 %collective-permute-start.3 = (bf16[96,512]{1,0:T(8,128)(2,1)S(1)}, bf16[96,512]{1,0:T(8,128)(2,1)S(1)}, u32[]{:S(2)}, u32[]{:S(2)}) collective-permute-start(bf16[96,512]{1,0:T(8,128)(2,1)S(1)} %collective-permute-done.2), channel_id=1, source_target_pairs={{0,1},{1,2},{2,3},{3,4},{4,5},{5,6},{6,7},{7,8},{8,9},{9,10},{10,1... | collective-permute-start | bytes 294920 | tf_op jit(solution)/shard_map/ppermute | solution.py:14
  52.5 8.8 %collective-permute-start.4 = (bf16[96,512]{1,0:T(8,128)(2,1)S(1)}, bf16[96,512]{1,0:T(8,128)(2,1)S(1)}, u32[]{:S(2)}, u32[]{:S(2)}) collective-permute-start(bf16[96,512]{1,0:T(8,128)(2,1)S(1)} %collective-permute-done.3), channel_id=1, source_target_pairs={{0,1},{1,2},{2,3},{3,4},{4,5},{5,6},{6,7},{7,8},{8,9},{9,10},{10,1... | collective-permute-start | bytes 294920 | tf_op jit(solution)/shard_map/ppermute | solution.py:14
  61.3 8.9 %collective-permute-start.5 = (bf16[96,512]{1,0:T(8,128)(2,1)S(1)}, bf16[96,512]{1,0:T(8,128)(2,1)S(1)}, u32[]{:S(2)}, u32[]{:S(2)}) collective-permute-start(bf16[96,512]{1,0:T(8,128)(2,1)S(1)} %collective-permute-done.4), channel_id=1, source_target_pairs={{0,1},{1,2},{2,3},{3,4},{4,5},{5,6},{6,7},{7,8},{8,9},{9,10},{10,1... | collective-permute-start | bytes 294920 | tf_op jit(solution)/shard_map/ppermute | solution.py:14
  70.2 9.0 %collective-permute-start.6 = (bf16[96,512]{1,0:T(8,128)(2,1)S(1)}, bf16[96,512]{1,0:T(8,128)(2,1)S(1)}, u32[]{:S(2)}, u32[]{:S(2)}) collective-permute-start(bf16[96,512]{1,0:T(8,128)(2,1)S(1)} %collective-permute-done.5), channel_id=1, source_target_pairs={{0,1},{1,2},{2,3},{3,4},{4,5},{5,6},{6,7},{7,8},{8,9},{9,10},{10,1... | collective-permute-start | bytes 294920 | tf_op jit(solution)/shard_map/ppermute | solution.py:14
  79.2 9.1 %collective-permute-start.7 = (bf16[96,512]{1,0:T(8,128)(2,1)S(1)}, bf16[96,512]{1,0:T(8,128)(2,1)S(1)}, u32[]{:S(2)}, u32[]{:S(2)}) collective-permute-start(bf16[96,512]{1,0:T(8,128)(2,1)S(1)} %collective-permute-done.6), channel_id=1, source_target_pairs={{0,1},{1,2},{2,3},{3,4},{4,5},{5,6},{6,7},{7,8},{8,9},{9,10},{10,1... | collective-permute-start | bytes 294920 | tf_op jit(solution)/shard_map/ppermute | solution.py:14
  88.3 9.0 %collective-permute-start.8 = (bf16[96,512]{1,0:T(8,128)(2,1)S(1)}, bf16[96,512]{1,0:T(8,128)(2,1)S(1)}, u32[]{:S(2)}, u32[]{:S(2)}) collective-permute-start(bf16[96,512]{1,0:T(8,128)(2,1)S(1)} %collective-permute-done.7), channel_id=1, source_target_pairs={{0,1},{1,2},{2,3},{3,4},{4,5},{5,6},{6,7},{7,8},{8,9},{9,10},{10,1... | collective-permute-start | bytes 294920 | tf_op jit(solution)/shard_map/ppermute | solution.py:14
  97.3 6.8 %collective-permute-start.9 = (bf16[96,512]{1,0:T(8,128)(2,1)S(1)}, bf16[96,512]{1,0:T(8,128)(2,1)S(1)}, u32[]{:S(2)}, u32[]{:S(2)}) collective-permute-start(bf16[96,512]{1,0:T(8,128)(2,1)S(1)} %collective-permute-done.8), channel_id=1, source_target_pairs={{0,1},{1,2},{2,3},{3,4},{4,5},{5,6},{6,7},{7,8},{8,9},{9,10},{10,1... | collective-permute-start | bytes 294920 | tf_op jit(solution)/shard_map/ppermute | solution.py:14
  104.1 6.7 %collective-permute-start.10 = (bf16[96,512]{1,0:T(8,128)(2,1)S(1)}, bf16[96,512]{1,0:T(8,128)(2,1)S(1)}, u32[]{:S(2)}, u32[]{:S(2)}) collective-permute-start(bf16[96,512]{1,0:T(8,128)(2,1)S(1)} %collective-permute-done.9), channel_id=1, source_target_pairs={{0,1},{1,2},{2,3},{3,4},{4,5},{5,6},{6,7},{7,8},{8,9},{9,10},{10,1... | collective-permute-start | bytes 294920 | tf_op jit(solution)/shard_map/ppermute | solution.py:14
  110.9 7.0 %collective-permute-start.11 = (bf16[96,512]{1,0:T(8,128)(2,1)S(1)}, bf16[96,512]{1,0:T(8,128)(2,1)S(1)}, u32[]{:S(2)}, u32[]{:S(2)}) collective-permute-start(bf16[96,512]{1,0:T(8,128)(2,1)S(1)} %collective-permute-done.10), channel_id=1, source_target_pairs={{0,1},{1,2},{2,3},{3,4},{4,5},{5,6},{6,7},{7,8},{8,9},{9,10},{10,1... | collective-permute-start | bytes 294920 | tf_op jit(solution)/shard_map/ppermute | solution.py:14
  117.8 8.9 %collective-permute-start.12 = (bf16[96,512]{1,0:T(8,128)(2,1)S(1)}, bf16[96,512]{1,0:T(8,128)(2,1)S(1)}, u32[]{:S(2)}, u32[]{:S(2)}) collective-permute-start(bf16[96,512]{1,0:T(8,128)(2,1)S(1)} %collective-permute-done.11), channel_id=1, source_target_pairs={{0,1},{1,2},{2,3},{3,4},{4,5},{5,6},{6,7},{7,8},{8,9},{9,10},{10,1... | collective-permute-start | bytes 294920 | tf_op jit(solution)/shard_map/ppermute | solution.py:14
  126.7 9.0 %collective-permute-start.13 = (bf16[96,512]{1,0:T(8,128)(2,1)S(1)}, bf16[96,512]{1,0:T(8,128)(2,1)S(1)}, u32[]{:S(2)}, u32[]{:S(2)}) collective-permute-start(bf16[96,512]{1,0:T(8,128)(2,1)S(1)} %collective-permute-done.12), channel_id=1, source_target_pairs={{0,1},{1,2},{2,3},{3,4},{4,5},{5,6},{6,7},{7,8},{8,9},{9,10},{10,1... | collective-permute-start | bytes 294920 | tf_op jit(solution)/shard_map/ppermute | solution.py:14
  135.7 6.7 %collective-permute-start.14 = (bf16[96,512]{1,0:T(8,128)(2,1)S(1)}, bf16[96,512]{1,0:T(8,128)(2,1)S(1)}, u32[]{:S(2)}, u32[]{:S(2)}) collective-permute-start(bf16[96,512]{1,0:T(8,128)(2,1)S(1)} %collective-permute-done.13), channel_id=1, source_target_pairs={{0,1},{1,2},{2,3},{3,4},{4,5},{5,6},{6,7},{7,8},{8,9},{9,10},{10,1... | collective-permute-start | bytes 294920 | tf_op jit(solution)/shard_map/ppermute | solution.py:14
  173.9 8.8 %collective-permute-start.15 = (bf16[96,512]{1,0:T(8,128)(2,1)S(1)}, bf16[96,512]{1,0:T(8,128)(2,1)S(1)}, u32[]{:S(2)}, u32[]{:S(2)}) collective-permute-start(bf16[96,512]{1,0:T(8,128)(2,1)S(1)} %get-tuple-element.10), channel_id=1, source_target_pairs={{0,1},{1,2},{2,3},{3,4},{4,5},{5,6},{6,7},{7,8},{8,9},{9,10},{10,1... | collective-permute-start | bytes 294920 | tf_op jit(solution)/shard_map/ppermute | solution.py:14
  182.7 8.8 %collective-permute-start.16 = (bf16[96,512]{1,0:T(8,128)(2,1)S(1)}, bf16[96,512]{1,0:T(8,128)(2,1)S(1)}, u32[]{:S(2)}, u32[]{:S(2)}) collective-permute-start(bf16[96,512]{1,0:T(8,128)(2,1)S(1)} %collective-permute-done.15), channel_id=1, source_target_pairs={{0,1},{1,2},{2,3},{3,4},{4,5},{5,6},{6,7},{7,8},{8,9},{9,10},{10,1... | collective-permute-start | bytes 294920 | tf_op jit(solution)/shard_map/ppermute | solution.py:14
  191.5 9.1 %collective-permute-start.17 = (bf16[96,512]{1,0:T(8,128)(2,1)S(1)}, bf16[96,512]{1,0:T(8,128)(2,1)S(1)}, u32[]{:S(2)}, u32[]{:S(2)}) collective-permute-start(bf16[96,512]{1,0:T(8,128)(2,1)S(1)} %collective-permute-done.16), channel_id=1, source_target_pairs={{0,1},{1,2},{2,3},{3,4},{4,5},{5,6},{6,7},{7,8},{8,9},{9,10},{10,1... | collective-permute-start | bytes 294920 | tf_op jit(solution)/shard_map/ppermute | solution.py:14
  200.6 9.0 %collective-permute-start.18 = (bf16[96,512]{1,0:T(8,128)(2,1)S(1)}, bf16[96,512]{1,0:T(8,128)(2,1)S(1)}, u32[]{:S(2)}, u32[]{:S(2)}) collective-permute-start(bf16[96,512]{1,0:T(8,128)(2,1)S(1)} %collective-permute-done.17), channel_id=1, source_target_pairs={{0,1},{1,2},{2,3},{3,4},{4,5},{5,6},{6,7},{7,8},{8,9},{9,10},{10,1... | collective-permute-start | bytes 294920 | tf_op jit(solution)/shard_map/ppermute | solution.py:14
  209.6 9.1 %collective-permute-start.19 = (bf16[96,512]{1,0:T(8,128)(2,1)S(1)}, bf16[96,512]{1,0:T(8,128)(2,1)S(1)}, u32[]{:S(2)}, u32[]{:S(2)}) collective-permute-start(bf16[96,512]{1,0:T(8,128)(2,1)S(1)} %collective-permute-done.18), channel_id=1, source_target_pairs={{0,1},{1,2},{2,3},{3,4},{4,5},{5,6},{6,7},{7,8},{8,9},{9,10},{10,1... | collective-permute-start | bytes 294920 | tf_op jit(solution)/shard_map/ppermute | solution.py:14
  218.6 6.8 %collective-permute-start.20 = (bf16[96,512]{1,0:T(8,128)(2,1)S(1)}, bf16[96,512]{1,0:T(8,128)(2,1)S(1)}, u32[]{:S(2)}, u32[]{:S(2)}) collective-permute-start(bf16[96,512]{1,0:T(8,128)(2,1)S(1)} %collective-permute-done.19), channel_id=1, source_target_pairs={{0,1},{1,2},{2,3},{3,4},{4,5},{5,6},{6,7},{7,8},{8,9},{9,10},{10,1... | collective-permute-start | bytes 294920 | tf_op jit(solution)/shard_map/ppermute | solution.py:14
  225.5 6.7 %collective-permute-start.21 = (bf16[96,512]{1,0:T(8,128)(2,1)S(1)}, bf16[96,512]{1,0:T(8,128)(2,1)S(1)}, u32[]{:S(2)}, u32[]{:S(2)}) collective-permute-start(bf16[96,512]{1,0:T(8,128)(2,1)S(1)} %collective-permute-done.20), channel_id=1, source_target_pairs={{0,1},{1,2},{2,3},{3,4},{4,5},{5,6},{6,7},{7,8},{8,9},{9,10},{10,1... | collective-permute-start | bytes 294920 | tf_op jit(solution)/shard_map/ppermute | solution.py:14
  232.2 6.7 %collective-permute-start.22 = (bf16[96,512]{1,0:T(8,128)(2,1)S(1)}, bf16[96,512]{1,0:T(8,128)(2,1)S(1)}, u32[]{:S(2)}, u32[]{:S(2)}) collective-permute-start(bf16[96,512]{1,0:T(8,128)(2,1)S(1)} %collective-permute-done.21), channel_id=1, source_target_pairs={{0,1},{1,2},{2,3},{3,4},{4,5},{5,6},{6,7},{7,8},{8,9},{9,10},{10,1... | collective-permute-start | bytes 294920 | tf_op jit(solution)/shard_map/ppermute | solution.py:14
  239.0 8.8 %collective-permute-start.23 = (bf16[96,512]{1,0:T(8,128)(2,1)S(1)}, bf16[96,512]{1,0:T(8,128)(2,1)S(1)}, u32[]{:S(2)}, u32[]{:S(2)}) collective-permute-start(bf16[96,512]{1,0:T(8,128)(2,1)S(1)} %collective-permute-done.22), channel_id=1, source_target_pairs={{0,1},{1,2},{2,3},{3,4},{4,5},{5,6},{6,7},{7,8},{8,9},{9,10},{10,1... | collective-permute-start | bytes 294920 | tf_op jit(solution)/shard_map/ppermute | solution.py:14
  247.8 9.0 %collective-permute-start.24 = (bf16[96,512]{1,0:T(8,128)(2,1)S(1)}, bf16[96,512]{1,0:T(8,128)(2,1)S(1)}, u32[]{:S(2)}, u32[]{:S(2)}) collective-permute-start(bf16[96,512]{1,0:T(8,128)(2,1)S(1)} %collective-permute-done.23), channel_id=1, source_target_pairs={{0,1},{1,2},{2,3},{3,4},{4,5},{5,6},{6,7},{7,8},{8,9},{9,10},{10,1... | collective-permute-start | bytes 294920 | tf_op jit(solution)/shard_map/ppermute | solution.py:14
  256.8 7.2 %collective-permute-start.25 = (bf16[96,512]{1,0:T(8,128)(2,1)S(1)}, bf16[96,512]{1,0:T(8,128)(2,1)S(1)}, u32[]{:S(2)}, u32[]{:S(2)}) collective-permute-start(bf16[96,512]{1,0:T(8,128)(2,1)S(1)} %collective-permute-done.24), channel_id=1, source_target_pairs={{0,1},{1,2},{2,3},{3,4},{4,5},{5,6},{6,7},{7,8},{8,9},{9,10},{10,1... | collective-permute-start | bytes 294920 | tf_op jit(solution)/shard_map/ppermute | solution.py:14
  264.0 6.7 %collective-permute-start.26 = (bf16[96,512]{1,0:T(8,128)(2,1)S(1)}, bf16[96,512]{1,0:T(8,128)(2,1)S(1)}, u32[]{:S(2)}, u32[]{:S(2)}) collective-permute-start(bf16[96,512]{1,0:T(8,128)(2,1)S(1)} %collective-permute-done.25), channel_id=1, source_target_pairs={{0,1},{1,2},{2,3},{3,4},{4,5},{5,6},{6,7},{7,8},{8,9},{9,10},{10,1... | collective-permute-start | bytes 294920 | tf_op jit(solution)/shard_map/ppermute | solution.py:14
  270.8 6.7 %collective-permute-start.27 = (bf16[96,512]{1,0:T(8,128)(2,1)S(1)}, bf16[96,512]{1,0:T(8,128)(2,1)S(1)}, u32[]{:S(2)}, u32[]{:S(2)}) collective-permute-start(bf16[96,512]{1,0:T(8,128)(2,1)S(1)} %collective-permute-done.26), channel_id=1, source_target_pairs={{0,1},{1,2},{2,3},{3,4},{4,5},{5,6},{6,7},{7,8},{8,9},{9,10},{10,1... | collective-permute-start | bytes 294920 | tf_op jit(solution)/shard_map/ppermute | solution.py:14
  277.5 6.7 %collective-permute-start.28 = (bf16[96,512]{1,0:T(8,128)(2,1)S(1)}, bf16[96,512]{1,0:T(8,128)(2,1)S(1)}, u32[]{:S(2)}, u32[]{:S(2)}) collective-permute-start(bf16[96,512]{1,0:T(8,128)(2,1)S(1)} %collective-permute-done.27), channel_id=1, source_target_pairs={{0,1},{1,2},{2,3},{3,4},{4,5},{5,6},{6,7},{7,8},{8,9},{9,10},{10,1... | collective-permute-start | bytes 294920 | tf_op jit(solution)/shard_map/ppermute | solution.py:14
  284.2 6.7 %collective-permute-start.29 = (bf16[96,512]{1,0:T(8,128)(2,1)S(1)}, bf16[96,512]{1,0:T(8,128)(2,1)S(1)}, u32[]{:S(2)}, u32[]{:S(2)}) collective-permute-start(bf16[96,512]{1,0:T(8,128)(2,1)S(1)} %collective-permute-done.28), channel_id=1, source_target_pairs={{0,1},{1,2},{2,3},{3,4},{4,5},{5,6},{6,7},{7,8},{8,9},{9,10},{10,1... | collective-permute-start | bytes 294920 | tf_op jit(solution)/shard_map/ppermute | solution.py:14
Sparse Core Ops, SparseCore 0:
  15.6 119.8 reduce-scatter.4
  140.1 119.2 reduce-scatter.2
